TPU v7x, 512 devices: a whole 4x8x8 slice. The times are simulated.
512 devices in a mesh: grid: 64 (over x, z, core), orb: 8 (over y).
Axes of the slice: x: 4, y: 8, z: 8, core: 2. Of those that a mesh axis runs over, the one named last changes fastest.
Arguments:
- orbitals: float32 [256, 16, 16, 1024], P('grid', None, None, 'orb'), may hold values from -15 to 15
- potential: float32 [256, 16, 16], P('grid'), may hold values from -2 to 0
Outputs:
- filtered: float32 [256, 16, 16, 1024], P('grid', None, None, 'orb')
- hamiltonian_block: float32 [1024, 1024], P('orb', 'grid')
- margin_block: float32 [1024, 1024], P('orb', 'grid')
All inputs are finite; a program needn't handle non-finite values.
Results may differ from a plain program's by a relative error of at most 0.0039.
Values may be sent and summed in bfloat16 or wider, within the bound.
No kernel may reach another device: no remote copies, remote signals or barrier semaphores. Data moves between devices by JAX's collectives and lax.ppermute only.
A program may use at most 64 MiB of HBM per device.

v0:
```python
import jax
import jax.numpy as jnp
from jax import lax
from jax.sharding import PartitionSpec as P

DEGREE = 4
STENCIL = (-205.0 / 72.0, 8.0 / 5.0, -1.0 / 5.0, 8.0 / 315.0, -1.0 / 560.0)
LOWER_EDGE = -2.0
CUT_EDGE = 1.5
UPPER_EDGE = 10.0
EPSILON = 1e-06


def padded_2(shard, sides, width):
    for axis, dim in sides:
        size, length = (lax.axis_size(axis), shard.shape[dim])
        up = [(i, (i + 1) % size) for i in range(size - 1)]
        down = [(j, i) for i, j in up]
        last = lax.slice_in_dim(shard, length - width, length, axis=dim)
        initial = lax.slice_in_dim(shard, 0, width, axis=dim)
        before = lax.ppermute(last, axis, up)
        after = lax.ppermute(initial, axis, down)
        shard = jnp.concatenate([before, shard, after], axis=dim)
    return shard


def plane_matrix(rows_y, cols_x):
    flat_count = rows_y * cols_x
    index_all = jnp.arange(flat_count, dtype=jnp.int32)
    row_y = (index_all // cols_x)[:, None]
    row_x = (index_all % cols_x)[:, None]
    col_y = (index_all // cols_x)[None, :]
    col_x = (index_all % cols_x)[None, :]
    delta_y = jnp.mod(row_y - col_y, rows_y)
    delta_x = jnp.mod(row_x - col_x, cols_x)
    same_y = delta_y == 0
    same_x = delta_x == 0
    matrix = jnp.zeros((flat_count, flat_count), jnp.float32)
    for offset in range(1, 5):
        for signed in (offset, -offset):
            hit_y = jnp.logical_and(same_x, delta_y == signed % rows_y)
            hit_x = jnp.logical_and(same_y, delta_x == signed % cols_x)
            matrix = matrix + STENCIL[offset] * (
                hit_y.astype(jnp.float32) + hit_x.astype(jnp.float32)
            )
    return matrix


def apply_hamiltonian(current, potential, plane):
    layers, rows_y, cols_x, width = current.shape
    padded = padded_2(current.astype(jnp.bfloat16), (("grid", 0),), 4).astype(current.dtype)
    laplacian = 3.0 * STENCIL[0] * current
    for offset in range(1, 5):
        laplacian = laplacian + STENCIL[offset] * (
            padded[4 + offset : 4 + offset + layers] + padded[4 - offset : 4 - offset + layers]
        )
    flat = current.reshape(layers, rows_y * cols_x, width)
    in_plane = jnp.einsum(
        "pq,zqo->zpo",
        plane,
        flat,
        precision=lax.Precision.HIGHEST,
        preferred_element_type=jnp.float32,
    )
    laplacian = laplacian + in_plane.reshape(current.shape)
    return -0.5 * laplacian + potential[:, :, :, None] * current


def chebyshev(initial, potential, plane):
    half_width = (UPPER_EDGE - CUT_EDGE) / 2.0
    centre = (UPPER_EDGE + CUT_EDGE) / 2.0
    sigma_now = half_width / (LOWER_EDGE - centre)
    gamma_ratio = 2.0 / sigma_now
    previous = initial
    current = (
        sigma_now / half_width * (apply_hamiltonian(previous, potential, plane) - centre * previous)
    )
    for degree_step in range(DEGREE - 1):
        sigma_next = 1.0 / (gamma_ratio - sigma_now)
        following = (
            2.0
            * sigma_next
            / half_width
            * (apply_hamiltonian(current, potential, plane) - centre * current)
            - sigma_now * sigma_next * previous
        )
        previous, current, sigma_now = (current, following, sigma_next)
    return current


def contract_points(left_side, right_side):
    return lax.dot_general(
        left_side, right_side, (((0,), (0,)), ((), ())), preferred_element_type=jnp.float32
    )


def on_device(orbitals, potential):
    own_width = orbitals.shape[3]
    point_count = orbitals.shape[0] * orbitals.shape[1] * orbitals.shape[2]
    point_total = float(point_count * lax.axis_size("grid"))
    plane = plane_matrix(orbitals.shape[1], orbitals.shape[2])
    result_block = chebyshev(orbitals, potential, plane)
    own_squares = jnp.sum(result_block * result_block, axis=(0, 1, 2))
    rounded_orbitals = result_block.astype(jnp.bfloat16).reshape(point_count, own_width)
    rounded_image = (
        apply_hamiltonian(result_block, potential, plane)
        .astype(jnp.bfloat16)
        .reshape(point_count, own_width)
    )
    summed_own = lax.psum(own_squares, "grid")
    squares_all = lax.all_gather(summed_own, "orb", axis=0, tiled=True)
    scale_all = 1.0 / jnp.sqrt(squares_all / point_total + EPSILON)
    scale_own = lax.dynamic_slice_in_dim(scale_all, lax.axis_index("orb") * own_width, own_width)
    filtered = result_block * scale_own
    orbitals_all, images_all = (
        lax.all_gather(rounded_orbitals, "orb", axis=1, tiled=True),
        lax.all_gather(rounded_image, "orb", axis=1, tiled=True),
    )
    hamiltonian_part = contract_points(images_all, rounded_orbitals)
    margin_part = contract_points(orbitals_all, rounded_orbitals)
    combined = lax.psum_scatter(
        jnp.concatenate([hamiltonian_part, margin_part], axis=1),
        "grid",
        scatter_dimension=0,
        tiled=True,
    )
    column_count = combined.shape[0]
    column_scale = lax.dynamic_slice_in_dim(
        scale_all, lax.axis_index("grid") * column_count, column_count
    )
    pair_scale = scale_own[:, None] * column_scale[None, :] / point_total
    hamiltonian_block = combined[:, :own_width].T * pair_scale
    margin_block = combined[:, own_width:].T * pair_scale
    return (filtered, hamiltonian_block, margin_block)


def solution(mesh):
    placed = (P("grid", None, None, "orb"), P("grid", None, None))
    return jax.shard_map(
        on_device,
        mesh=mesh,
        in_specs=placed,
        out_specs=(P("grid", None, None, "orb"), P("orb", "grid"), P("orb", "grid")),
        check_vma=False,
    )
```

profile of v0, /device:TPU:8, one launch (start us, length us, event | category | flops | bytes accessed | tf_op | source)
XLA Modules:
  0.0 412.1 jit_solution(13175780743739567016)
XLA Ops:
  7.2 1.1 convert_element_type.210
  8.3 1.3 collective-permute-start.1
  9.6 3.0 collective-permute-start
  12.7 0.8 broadcast_multiply_fusion.2
  13.4 2.7 fusion.72
  16.3 0.9 copy-done.1
  17.5 1.3 collective-permute-start.3
  18.8 4.5 %collective-permute-start.2 = (bf16[4,16,16,128]{3,2,1,0:T(8,128)(2,1)S(1)}, bf16[4,16,16,128]{3,2,1,0:T(8,128)(2,1)S(1)}, u32[]{:S(2)}, u32[]{:S(2)}) collective-permute-start(bf16[4,16,16,128]{3,2,1,0:T(8,128)(2,1)S(1)} %get-tuple-element.18), channel_id=1, source_target_pairs={{0,8},{8,16},{16,24},{24,32},{32,40},{40,48},{48,56},{56,64},{64,7... | collective-permute-start | bytes 786440 | tf_op jit(solution)/shard_map/ppermute | solution.py:21
  23.4 1.9 convolution_bitcast_fusion.3
  25.7 0.4 fusion.160
  26.2 1.3 collective-permute-start.5
  27.5 5.3 %collective-permute-start.4 = (bf16[4,16,16,128]{3,2,1,0:T(8,128)(2,1)S(1)}, bf16[4,16,16,128]{3,2,1,0:T(8,128)(2,1)S(1)}, u32[]{:S(2)}, u32[]{:S(2)}) collective-permute-start(bf16[4,16,16,128]{3,2,1,0:T(8,128)(2,1)S(1)} %get-tuple-element.16), channel_id=1, source_target_pairs={{0,8},{8,16},{16,24},{24,32},{32,40},{40,48},{48,56},{56,64},{64,7... | collective-permute-start | bytes 786440 | tf_op jit(solution)/shard_map/ppermute | solution.py:21
  32.8 1.9 convolution_bitcast_fusion.2
  35.1 0.4 fusion.158
  35.5 1.3 collective-permute-start.7
  36.8 6.2 %collective-permute-start.6 = (bf16[4,16,16,128]{3,2,1,0:T(8,128)(2,1)S(1)}, bf16[4,16,16,128]{3,2,1,0:T(8,128)(2,1)S(1)}, u32[]{:S(2)}, u32[]{:S(2)}) collective-permute-start(bf16[4,16,16,128]{3,2,1,0:T(8,128)(2,1)S(1)} %get-tuple-element.14), channel_id=1, source_target_pairs={{0,8},{8,16},{16,24},{24,32},{32,40},{40,48},{48,56},{56,64},{64,7... | collective-permute-start | bytes 786440 | tf_op jit(solution)/shard_map/ppermute | solution.py:21
  43.0 1.9 convolution_bitcast_fusion.1
  45.3 1.2 fusion.156
  46.5 1.3 collective-permute-start.9
  47.8 6.3 %collective-permute-start.8 = (bf16[4,16,16,128]{3,2,1,0:T(8,128)(2,1)}, bf16[4,16,16,128]{3,2,1,0:T(8,128)(2,1)S(1)}, u32[]{:S(2)}, u32[]{:S(2)}) collective-permute-start(bf16[4,16,16,128]{3,2,1,0:T(8,128)(2,1)} %get-tuple-element.12), channel_id=1, source_target_pairs={{0,8},{8,16},{16,24},{24,32},{32,40},{40,48},{48,56},{56,64},{64,7... | collective-permute-start | bytes 786440 | tf_op jit(solution)/shard_map/ppermute | solution.py:21
  54.1 1.9 convolution_bitcast_fusion
  56.4 134.8 %psum.7 = f32[128]{0:T(128)S(1)} all-reduce(f32[128]{0:T(128)S(1)} %multiply_reduce_fusion), channel_id=1, replica_groups=mesh['grid'=64,'orb'=8] {'grid'}, use_global_device_ids=true, to_apply=%region_1.2 | all-reduce | flops 128 | bytes 1024 | tf_op jit(solution)/shard_map/psum | solution.py:110
  191.2 15.3 %all-gather = f32[8,1,128]{2,1,0:T(1,128)S(1)} all-gather(f32[1,1,128]{2,1,0:T(1,128)S(1)} %bitcast.65), channel_id=1, replica_groups=mesh['grid'=64,'orb'=8] {'orb'}, dimensions={0}, use_global_device_ids=true | all-gather | bytes 4608 | tf_op jit(solution)/shard_map/all_gather | solution.py:111
  206.7 1.3 fusion.5
  208.1 2.1 fusion.165
  210.2 39.9 %all-gather.4.cloned.1.call-done = bf16[1024,1024]{1,0:T(8,128)(2,1)} async-done(((bf16[1024,128]{1,0:T(8,128)(2,1)}), bf16[1024,1024]{1,0:T(8,128)(2,1)}) %all-gather.4.cloned.1.call-update) | async-done | bytes 2097168 | tf_op jit(solution)/shard_map/all_gather | solution.py:117
  250.1 2.1 fusion.164
  252.2 1.3 copy.39
  253.7 149.6 %reduce-scatter.4.cloned.1.call-done = f32[16,256]{1,0:T(8,128)} async-done(((f32[1024,256]{1,0:T(8,128)}), f32[16,256]{1,0:T(8,128)}) %reduce-scatter.4.cloned.1.call-update) | async-done | bytes 16400
  403.3 0.7 fusion.163
  404.3 0.7 copy.33
  404.9 0.7 copy.34
  (42 shorter events, 2.7 us)
Async XLA Ops:
  7.2 200.9 %all-gather.6.cloned.1.call-start = ((), (), s32[]{:S(2)}) async-start(), calls=%async_computation.2 | async-start | bytes 2359296 | tf_op jit(solution)/shard_map/all_gather | solution.py:116
  8.3 7.8 %collective-permute-start.1 = (bf16[4,16,16,128]{3,2,1,0:T(8,128)(2,1)S(1)}, bf16[4,16,16,128]{3,2,1,0:T(8,128)(2,1)S(1)}, u32[]{:S(2)}, u32[]{:S(2)}) collective-permute-start(bf16[4,16,16,128]{3,2,1,0:T(8,128)(2,1)S(1)} %convert_element_type.210), channel_id=1, source_target_pairs={{8,0},{16,8},{24,16},{32,24},{40,32},{48,40},{56,48},{64,56},{72,6... | collective-permute-start | bytes 786440 | tf_op jit(solution)/shard_map/ppermute | solution.py:22
  9.6 6.5 %collective-permute-start = (bf16[4,16,16,128]{3,2,1,0:T(8,128)(2,1)S(1)}, bf16[4,16,16,128]{3,2,1,0:T(8,128)(2,1)S(1)}, u32[]{:S(2)}, u32[]{:S(2)}) collective-permute-start(bf16[4,16,16,128]{3,2,1,0:T(8,128)(2,1)S(1)} %convert_element_type.210), channel_id=1, source_target_pairs={{0,8},{8,16},{16,24},{24,32},{32,40},{40,48},{48,56},{56,64},{64,7... | collective-permute-start | bytes 786440 | tf_op jit(solution)/shard_map/ppermute | solution.py:21
  16.1 1.0 copy-start.1
  16.1 1.0 copy-start.2
  17.5 8.0 %collective-permute-start.3 = (bf16[4,16,16,128]{3,2,1,0:T(8,128)(2,1)S(1)}, bf16[4,16,16,128]{3,2,1,0:T(8,128)(2,1)S(1)}, u32[]{:S(2)}, u32[]{:S(2)}) collective-permute-start(bf16[4,16,16,128]{3,2,1,0:T(8,128)(2,1)S(1)} %get-tuple-element.18), channel_id=1, source_target_pairs={{8,0},{16,8},{24,16},{32,24},{40,32},{48,40},{56,48},{64,56},{72,6... | collective-permute-start | bytes 786440 | tf_op jit(solution)/shard_map/ppermute | solution.py:22
  18.8 6.7 %collective-permute-start.2 = (bf16[4,16,16,128]{3,2,1,0:T(8,128)(2,1)S(1)}, bf16[4,16,16,128]{3,2,1,0:T(8,128)(2,1)S(1)}, u32[]{:S(2)}, u32[]{:S(2)}) collective-permute-start(bf16[4,16,16,128]{3,2,1,0:T(8,128)(2,1)S(1)} %get-tuple-element.18), channel_id=1, source_target_pairs={{0,8},{8,16},{16,24},{24,32},{32,40},{40,48},{48,56},{56,64},{64,7... | collective-permute-start | bytes 786440 | tf_op jit(solution)/shard_map/ppermute | solution.py:21
  26.2 8.8 %collective-permute-start.5 = (bf16[4,16,16,128]{3,2,1,0:T(8,128)(2,1)S(1)}, bf16[4,16,16,128]{3,2,1,0:T(8,128)(2,1)S(1)}, u32[]{:S(2)}, u32[]{:S(2)}) collective-permute-start(bf16[4,16,16,128]{3,2,1,0:T(8,128)(2,1)S(1)} %get-tuple-element.16), channel_id=1, source_target_pairs={{8,0},{16,8},{24,16},{32,24},{40,32},{48,40},{56,48},{64,56},{72,6... | collective-permute-start | bytes 786440 | tf_op jit(solution)/shard_map/ppermute | solution.py:22
  27.5 7.5 %collective-permute-start.4 = (bf16[4,16,16,128]{3,2,1,0:T(8,128)(2,1)S(1)}, bf16[4,16,16,128]{3,2,1,0:T(8,128)(2,1)S(1)}, u32[]{:S(2)}, u32[]{:S(2)}) collective-permute-start(bf16[4,16,16,128]{3,2,1,0:T(8,128)(2,1)S(1)} %get-tuple-element.16), channel_id=1, source_target_pairs={{0,8},{8,16},{16,24},{24,32},{32,40},{40,48},{48,56},{56,64},{64,7... | collective-permute-start | bytes 786440 | tf_op jit(solution)/shard_map/ppermute | solution.py:21
  35.5 9.6 %collective-permute-start.7 = (bf16[4,16,16,128]{3,2,1,0:T(8,128)(2,1)S(1)}, bf16[4,16,16,128]{3,2,1,0:T(8,128)(2,1)S(1)}, u32[]{:S(2)}, u32[]{:S(2)}) collective-permute-start(bf16[4,16,16,128]{3,2,1,0:T(8,128)(2,1)S(1)} %get-tuple-element.14), channel_id=1, source_target_pairs={{8,0},{16,8},{24,16},{32,24},{40,32},{48,40},{56,48},{64,56},{72,6... | collective-permute-start | bytes 786440 | tf_op jit(solution)/shard_map/ppermute | solution.py:22
  36.8 8.3 %collective-permute-start.6 = (bf16[4,16,16,128]{3,2,1,0:T(8,128)(2,1)S(1)}, bf16[4,16,16,128]{3,2,1,0:T(8,128)(2,1)S(1)}, u32[]{:S(2)}, u32[]{:S(2)}) collective-permute-start(bf16[4,16,16,128]{3,2,1,0:T(8,128)(2,1)S(1)} %get-tuple-element.14), channel_id=1, source_target_pairs={{0,8},{8,16},{16,24},{24,32},{32,40},{40,48},{48,56},{56,64},{64,7... | collective-permute-start | bytes 786440 | tf_op jit(solution)/shard_map/ppermute | solution.py:21
  46.4 203.6 %all-gather.4.cloned.1.call-start = ((), (), s32[]{:S(2)}) async-start(), calls=%async_computation.1 | async-start | bytes 2359296 | tf_op jit(solution)/shard_map/all_gather | solution.py:117
  46.5 160.1 %collective-permute-start.9 = (bf16[4,16,16,128]{3,2,1,0:T(8,128)(2,1)}, bf16[4,16,16,128]{3,2,1,0:T(8,128)(2,1)S(1)}, u32[]{:S(2)}, u32[]{:S(2)}) collective-permute-start(bf16[4,16,16,128]{3,2,1,0:T(8,128)(2,1)} %get-tuple-element.12), channel_id=1, source_target_pairs={{8,0},{16,8},{24,16},{32,24},{40,32},{48,40},{56,48},{64,56},{72,6... | collective-permute-start | bytes 786440 | tf_op jit(solution)/shard_map/ppermute | solution.py:22
  47.8 158.8 %collective-permute-start.8 = (bf16[4,16,16,128]{3,2,1,0:T(8,128)(2,1)}, bf16[4,16,16,128]{3,2,1,0:T(8,128)(2,1)S(1)}, u32[]{:S(2)}, u32[]{:S(2)}) collective-permute-start(bf16[4,16,16,128]{3,2,1,0:T(8,128)(2,1)} %get-tuple-element.12), channel_id=1, source_target_pairs={{0,8},{8,16},{16,24},{24,32},{32,40},{40,48},{48,56},{56,64},{64,7... | collective-permute-start | bytes 786440 | tf_op jit(solution)/shard_map/ppermute | solution.py:21
  56.1 150.5 %copy-start = (bf16[4,16,16,128]{3,2,1,0:T(8,128)(2,1)S(1)}, bf16[4,16,16,128]{3,2,1,0:T(8,128)(2,1)}, u32[]{:S(2)}) copy-start(bf16[4,16,16,128]{3,2,1,0:T(8,128)(2,1)} %get-tuple-element.12) | copy-start | bytes 786436
  208.0 195.2 %reduce-scatter.4.cloned.1.call-start = ((), (), s32[]{:S(2)}) async-start(), calls=%async_computation.3 | async-start | bytes 1064960
Sparse Core Ops, SparseCore 0:
  46.6 66.5 all-gather.5
  208.2 41.8 all-gather.3
  254.6 148.5 reduce-scatter.3
where the time goes:
time: 413 us; the launch traced here: 412 us
  waiting for transfers between devices  190 us (46%)
  blocking collectives  150 us (36%)
  starting transfers between devices  32 us (8%)
  matrix products  14.5 us (4%)
  between operations  14.1 us (3%)
  other arithmetic  6.55 us (2%)
  local copies, waits for them, and re-layouts  5.38 us (1%)
    unnamed x4, waiting for transfers between devices  150 us
    psum x1, blocking collectives, on_device(): summed_own = lax.psum(own_squares, 'grid')  135 us
    all_gather x1, waiting for transfers between devices, on_device(): lax.all_gather(rounded_image, 'orb', axis=1, tiled=True)  39.9 us
    ppermute x5, starting transfers between devices, padded_2(): before = lax.ppermute(last, axis, up)  25.4 us
    all_gather x1, blocking collectives, on_device(): squares_all = lax.all_gather(summed_own, 'orb', axis=0, tiled=True)  15.3 us
    dot_general x5, matrix products, apply_hamiltonian(): jnp.einsum('pq,zqo->zpo', plane, flat, precision=lax.Precision.HIGHEST, p...  10.4 us
  transfers between devices with their start and end apart: 13, of which 2 were waited for; matrix products, arithmetic and copies ran while one was open for 4% of the time, Pallas kernels for 0%

commit v1 on v0

--- a/solution.py
+++ b/solution.py
@@ -9,6 +9,12 @@
 CUT_EDGE = 1.5
 UPPER_EDGE = 10.0
 EPSILON = 1e-06
+
+
+def in_order(pieces, dim):
+    pieces = jnp.moveaxis(pieces, 0, dim)
+    shape = pieces.shape
+    return pieces.reshape(*shape[:dim], shape[dim] * shape[dim + 1], *shape[dim + 2 :])
 
 
 def padded_2(shard, sides, width):
@@ -108,7 +114,19 @@
         .reshape(point_count, own_width)
     )
     summed_own = lax.psum(own_squares, "grid")
-    squares_all = lax.all_gather(summed_own, "orb", axis=0, tiled=True)
+    length_2 = lax.axis_size("orb")
+    pairs = [(i_2, (i_2 + 1) % length_2) for i_2 in range(length_2)]
+    back = [(b, a) for a, b in pairs]
+    lower, upper = ([], [])
+    for step in range(length_2 - 1):
+        if step % 2 == 0:
+            lower.append(lax.ppermute(lower[-1] if lower else summed_own, "orb", pairs))
+        else:
+            upper.append(lax.ppermute(upper[-1] if upper else summed_own, "orb", back))
+    tiles = jnp.stack([*lower[::-1], summed_own, *upper])
+    shift = lax.axis_index("orb") - len(lower)
+    tiles = tiles[(jnp.arange(length_2) - shift) % length_2]
+    squares_all = in_order(tiles, 0)
     scale_all = 1.0 / jnp.sqrt(squares_all / point_total + EPSILON)
     scale_own = lax.dynamic_slice_in_dim(scale_all, lax.axis_index("orb") * own_width, own_width)
     filtered = result_block * scale_own

time: 413 us -> 422 us (1.022)
  starting transfers between devices: 32 us -> 51.4 us
  blocking collectives: 150 us -> 135 us
    ppermute x0 -> x7, starting transfers between devices: none -> 22.7 us  [the longest x4 14.7 us: on_device(): lower.append(lax.ppermute(lower[-1] if lower else summed_own, 'orb', pairs))]
    all_gather x1 -> x0, blocking collectives: 15.3 us -> none  [on_device(): squares_all = lax.all_gather(summed_own, 'orb', axis=0, tiled=True)]
  transfers between devices with their start and end apart: 13 -> 20, of which waited for: 2 -> 3; matrix products, arithmetic and copies ran while one was open for 4% -> 4% of each run, Pallas kernels for 0% -> 0%
where the time goes in v1:
time: 422 us; the launch traced here: 421 us
  waiting for transfers between devices  194 us (46%)
  blocking collectives  135 us (32%)
  starting transfers between devices  51.4 us (12%)
  matrix products  14.5 us (3%)
  between operations  14.2 us (3%)
  other arithmetic  6.55 us (2%)
  local copies, waits for them, and re-layouts  5.99 us (1%)
    unnamed x4, waiting for transfers between devices  150 us
    psum x1, blocking collectives, on_device(): summed_own = lax.psum(own_squares, 'grid')  135 us
    all_gather x1, waiting for transfers between devices, on_device(): lax.all_gather(rounded_image, 'orb', axis=1, tiled=True)  43.7 us
    ppermute x5, starting transfers between devices, padded_2(): before = lax.ppermute(last, axis, up)  22.1 us
    ppermute x4, starting transfers between devices, on_device(): lower.append(lax.ppermute(lower[-1] if lower else summed_own, 'orb', pairs))  14.7 us
    dot_general x5, matrix products, apply_hamiltonian(): jnp.einsum('pq,zqo->zpo', plane, flat, precision=lax.Precision.HIGHEST, p...  10.4 us
  transfers between devices with their start and end apart: 20, of which 3 were waited for; matrix products, arithmetic and copies ran while one was open for 4% of the time, Pallas kernels for 0%

profile of v1, /device:TPU:8, one launch (start us, length us, event | category | flops | bytes accessed | tf_op | source)
XLA Modules:
  0.0 421.5 jit_solution(4004824662247317748)
XLA Ops:
  7.2 1.1 convert_element_type.210
  8.3 1.3 collective-permute-start.1
  9.6 3.0 collective-permute-start
  13.4 2.7 fusion.72
  16.3 0.9 copy-done.1
  17.5 1.3 collective-permute-start.3
  18.8 4.5 %collective-permute-start.2 = (bf16[4,16,16,128]{3,2,1,0:T(8,128)(2,1)S(1)}, bf16[4,16,16,128]{3,2,1,0:T(8,128)(2,1)S(1)}, u32[]{:S(2)}, u32[]{:S(2)}) collective-permute-start(bf16[4,16,16,128]{3,2,1,0:T(8,128)(2,1)S(1)} %get-tuple-element.18), channel_id=1, source_target_pairs={{0,8},{8,16},{16,24},{24,32},{32,40},{40,48},{48,56},{56,64},{64,7... | collective-permute-start | bytes 786440 | tf_op jit(solution)/shard_map/ppermute | solution.py:27
  23.4 1.9 convolution_bitcast_fusion.3
  26.2 1.3 collective-permute-start.5
  27.5 5.3 %collective-permute-start.4 = (bf16[4,16,16,128]{3,2,1,0:T(8,128)(2,1)S(1)}, bf16[4,16,16,128]{3,2,1,0:T(8,128)(2,1)S(1)}, u32[]{:S(2)}, u32[]{:S(2)}) collective-permute-start(bf16[4,16,16,128]{3,2,1,0:T(8,128)(2,1)S(1)} %get-tuple-element.16), channel_id=1, source_target_pairs={{0,8},{8,16},{16,24},{24,32},{32,40},{40,48},{48,56},{56,64},{64,7... | collective-permute-start | bytes 786440 | tf_op jit(solution)/shard_map/ppermute | solution.py:27
  32.8 1.9 convolution_bitcast_fusion.2
  35.5 1.3 collective-permute-start.7
  36.8 6.2 %collective-permute-start.6 = (bf16[4,16,16,128]{3,2,1,0:T(8,128)(2,1)S(1)}, bf16[4,16,16,128]{3,2,1,0:T(8,128)(2,1)S(1)}, u32[]{:S(2)}, u32[]{:S(2)}) collective-permute-start(bf16[4,16,16,128]{3,2,1,0:T(8,128)(2,1)S(1)} %get-tuple-element.14), channel_id=1, source_target_pairs={{0,8},{8,16},{16,24},{24,32},{32,40},{40,48},{48,56},{56,64},{64,7... | collective-permute-start | bytes 786440 | tf_op jit(solution)/shard_map/ppermute | solution.py:27
  43.0 1.9 convolution_bitcast_fusion.1
  45.3 1.1 fusion.158
  46.6 134.7 %psum.7 = f32[128]{0:T(128)S(1)} all-reduce(f32[128]{0:T(128)S(1)} %multiply_reduce_fusion), channel_id=1, replica_groups=mesh['grid'=64,'orb'=8] {'grid'}, use_global_device_ids=true, to_apply=%region_1.2 | all-reduce | flops 128 | bytes 1024 | tf_op jit(solution)/shard_map/psum | solution.py:116
  181.4 3.5 collective-permute-start.8
  184.9 2.4 collective-permute-start.12
  187.3 3.5 collective-permute-start.9
  190.8 2.4 collective-permute-start.13
  193.2 3.8 collective-permute-start.10
  197.0 1.3 collective-permute-start.16
  198.3 3.0 collective-permute-start.15
  201.4 3.3 collective-permute-start.14
  204.7 3.9 collective-permute-start.11
  208.6 1.9 convolution_bitcast_fusion
  212.2 1.3 fusion.5
  213.5 2.1 fusion.167
  215.6 43.7 %all-gather.3.cloned.1.call-done = bf16[1024,1024]{1,0:T(8,128)(2,1)} async-done(((bf16[1024,128]{1,0:T(8,128)(2,1)}), bf16[1024,1024]{1,0:T(8,128)(2,1)}) %all-gather.3.cloned.1.call-update) | async-done | bytes 2097168 | tf_op jit(solution)/shard_map/all_gather | solution.py:135
  259.4 2.1 fusion.166
  261.6 1.4 copy.39
  263.0 149.6 %reduce-scatter.4.cloned.1.call-done = f32[16,256]{1,0:T(8,128)} async-done(((f32[1024,256]{1,0:T(8,128)}), f32[16,256]{1,0:T(8,128)}) %reduce-scatter.4.cloned.1.call-update) | async-done | bytes 16400
  (59 shorter events, 7.6 us)
Async XLA Ops:
  7.2 206.4 %all-gather.5.cloned.1.call-start = ((), (), s32[]{:S(2)}) async-start(), calls=%async_computation.2 | async-start | bytes 2359296 | tf_op jit(solution)/shard_map/all_gather | solution.py:134
  8.3 7.8 %collective-permute-start.1 = (bf16[4,16,16,128]{3,2,1,0:T(8,128)(2,1)S(1)}, bf16[4,16,16,128]{3,2,1,0:T(8,128)(2,1)S(1)}, u32[]{:S(2)}, u32[]{:S(2)}) collective-permute-start(bf16[4,16,16,128]{3,2,1,0:T(8,128)(2,1)S(1)} %convert_element_type.210), channel_id=1, source_target_pairs={{8,0},{16,8},{24,16},{32,24},{40,32},{48,40},{56,48},{64,56},{72,6... | collective-permute-start | bytes 786440 | tf_op jit(solution)/shard_map/ppermute | solution.py:28
  9.6 6.5 %collective-permute-start = (bf16[4,16,16,128]{3,2,1,0:T(8,128)(2,1)S(1)}, bf16[4,16,16,128]{3,2,1,0:T(8,128)(2,1)S(1)}, u32[]{:S(2)}, u32[]{:S(2)}) collective-permute-start(bf16[4,16,16,128]{3,2,1,0:T(8,128)(2,1)S(1)} %convert_element_type.210), channel_id=1, source_target_pairs={{0,8},{8,16},{16,24},{24,32},{32,40},{40,48},{48,56},{56,64},{64,7... | collective-permute-start | bytes 786440 | tf_op jit(solution)/shard_map/ppermute | solution.py:27
  16.1 1.0 copy-start.1
  16.1 1.0 copy-start.2
  17.5 8.0 %collective-permute-start.3 = (bf16[4,16,16,128]{3,2,1,0:T(8,128)(2,1)S(1)}, bf16[4,16,16,128]{3,2,1,0:T(8,128)(2,1)S(1)}, u32[]{:S(2)}, u32[]{:S(2)}) collective-permute-start(bf16[4,16,16,128]{3,2,1,0:T(8,128)(2,1)S(1)} %get-tuple-element.18), channel_id=1, source_target_pairs={{8,0},{16,8},{24,16},{32,24},{40,32},{48,40},{56,48},{64,56},{72,6... | collective-permute-start | bytes 786440 | tf_op jit(solution)/shard_map/ppermute | solution.py:28
  18.8 6.7 %collective-permute-start.2 = (bf16[4,16,16,128]{3,2,1,0:T(8,128)(2,1)S(1)}, bf16[4,16,16,128]{3,2,1,0:T(8,128)(2,1)S(1)}, u32[]{:S(2)}, u32[]{:S(2)}) collective-permute-start(bf16[4,16,16,128]{3,2,1,0:T(8,128)(2,1)S(1)} %get-tuple-element.18), channel_id=1, source_target_pairs={{0,8},{8,16},{16,24},{24,32},{32,40},{40,48},{48,56},{56,64},{64,7... | collective-permute-start | bytes 786440 | tf_op jit(solution)/shard_map/ppermute | solution.py:27
  26.2 8.8 %collective-permute-start.5 = (bf16[4,16,16,128]{3,2,1,0:T(8,128)(2,1)S(1)}, bf16[4,16,16,128]{3,2,1,0:T(8,128)(2,1)S(1)}, u32[]{:S(2)}, u32[]{:S(2)}) collective-permute-start(bf16[4,16,16,128]{3,2,1,0:T(8,128)(2,1)S(1)} %get-tuple-element.16), channel_id=1, source_target_pairs={{8,0},{16,8},{24,16},{32,24},{40,32},{48,40},{56,48},{64,56},{72,6... | collective-permute-start | bytes 786440 | tf_op jit(solution)/shard_map/ppermute | solution.py:28
  27.5 7.5 %collective-permute-start.4 = (bf16[4,16,16,128]{3,2,1,0:T(8,128)(2,1)S(1)}, bf16[4,16,16,128]{3,2,1,0:T(8,128)(2,1)S(1)}, u32[]{:S(2)}, u32[]{:S(2)}) collective-permute-start(bf16[4,16,16,128]{3,2,1,0:T(8,128)(2,1)S(1)} %get-tuple-element.16), channel_id=1, source_target_pairs={{0,8},{8,16},{16,24},{24,32},{32,40},{40,48},{48,56},{56,64},{64,7... | collective-permute-start | bytes 786440 | tf_op jit(solution)/shard_map/ppermute | solution.py:27
  35.5 9.6 %collective-permute-start.7 = (bf16[4,16,16,128]{3,2,1,0:T(8,128)(2,1)S(1)}, bf16[4,16,16,128]{3,2,1,0:T(8,128)(2,1)S(1)}, u32[]{:S(2)}, u32[]{:S(2)}) collective-permute-start(bf16[4,16,16,128]{3,2,1,0:T(8,128)(2,1)S(1)} %get-tuple-element.14), channel_id=1, source_target_pairs={{8,0},{16,8},{24,16},{32,24},{40,32},{48,40},{56,48},{64,56},{72,6... | collective-permute-start | bytes 786440 | tf_op jit(solution)/shard_map/ppermute | solution.py:28
  36.8 8.3 %collective-permute-start.6 = (bf16[4,16,16,128]{3,2,1,0:T(8,128)(2,1)S(1)}, bf16[4,16,16,128]{3,2,1,0:T(8,128)(2,1)S(1)}, u32[]{:S(2)}, u32[]{:S(2)}) collective-permute-start(bf16[4,16,16,128]{3,2,1,0:T(8,128)(2,1)S(1)} %get-tuple-element.14), channel_id=1, source_target_pairs={{0,8},{8,16},{16,24},{24,32},{32,40},{40,48},{48,56},{56,64},{64,7... | collective-permute-start | bytes 786440 | tf_op jit(solution)/shard_map/ppermute | solution.py:27
  46.4 212.9 %all-gather.3.cloned.1.call-start = ((), (), s32[]{:S(2)}) async-start(), calls=%async_computation.1 | async-start | bytes 2359296 | tf_op jit(solution)/shard_map/all_gather | solution.py:135
  181.4 5.9 %collective-permute-start.8 = (f32[128]{0:T(128)S(1)}, f32[128]{0:T(128)S(1)}, u32[]{:S(2)}, u32[]{:S(2)}) collective-permute-start(f32[128]{0:T(128)S(1)} %psum.7), channel_id=1, source_target_pairs={{0,1},{1,2},{2,3},{3,4},{4,5},{5,6},{6,7},{7,0},{8,9},{9,10},{10,1... | collective-permute-start | bytes 1544 | tf_op jit(solution)/shard_map/ppermute | solution.py:123
  184.9 5.9 %collective-permute-start.12 = (f32[128]{0:T(128)S(1)}, f32[128]{0:T(128)S(1)}, u32[]{:S(2)}, u32[]{:S(2)}) collective-permute-start(f32[128]{0:T(128)S(1)} %psum.7), channel_id=1, source_target_pairs={{1,0},{2,1},{3,2},{4,3},{5,4},{6,5},{7,6},{0,7},{9,8},{10,9},{11,1... | collective-permute-start | bytes 1544 | tf_op jit(solution)/shard_map/ppermute | solution.py:125
  187.3 5.9 %collective-permute-start.9 = (f32[128]{0:T(128)S(1)}, f32[128]{0:T(128)S(1)}, u32[]{:S(2)}, u32[]{:S(2)}) collective-permute-start(f32[128]{0:T(128)S(1)} %collective-permute-done.8), channel_id=1, source_target_pairs={{0,1},{1,2},{2,3},{3,4},{4,5},{5,6},{6,7},{7,0},{8,9},{9,10},{10,1... | collective-permute-start | bytes 1544 | tf_op jit(solution)/shard_map/ppermute | solution.py:123
  190.8 10.6 %collective-permute-start.13 = (f32[128]{0:T(128)S(1)}, f32[128]{0:T(128)S(1)}, u32[]{:S(2)}, u32[]{:S(2)}) collective-permute-start(f32[128]{0:T(128)S(1)} %collective-permute-done.12), channel_id=1, source_target_pairs={{1,0},{2,1},{3,2},{4,3},{5,4},{6,5},{7,6},{0,7},{9,8},{10,9},{11,1... | collective-permute-start | bytes 1544 | tf_op jit(solution)/shard_map/ppermute | solution.py:125
  193.2 11.5 %collective-permute-start.10 = (f32[128]{0:T(128)S(1)}, f32[128]{0:T(128)S(1)}, u32[]{:S(2)}, u32[]{:S(2)}) collective-permute-start(f32[128]{0:T(128)S(1)} %collective-permute-done.9), channel_id=1, source_target_pairs={{0,1},{1,2},{2,3},{3,4},{4,5},{5,6},{6,7},{7,0},{8,9},{9,10},{10,1... | collective-permute-start | bytes 1544 | tf_op jit(solution)/shard_map/ppermute | solution.py:123
  197.0 15.0 %collective-permute-start.16 = (bf16[4,16,16,128]{3,2,1,0:T(8,128)(2,1)}, bf16[4,16,16,128]{3,2,1,0:T(8,128)(2,1)S(1)}, u32[]{:S(2)}, u32[]{:S(2)}) collective-permute-start(bf16[4,16,16,128]{3,2,1,0:T(8,128)(2,1)} %get-tuple-element.12), channel_id=1, source_target_pairs={{8,0},{16,8},{24,16},{32,24},{40,32},{48,40},{56,48},{64,56},{72,6... | collective-permute-start | bytes 786440 | tf_op jit(solution)/shard_map/ppermute | solution.py:28
  198.3 13.7 %collective-permute-start.15 = (bf16[4,16,16,128]{3,2,1,0:T(8,128)(2,1)}, bf16[4,16,16,128]{3,2,1,0:T(8,128)(2,1)S(1)}, u32[]{:S(2)}, u32[]{:S(2)}) collective-permute-start(bf16[4,16,16,128]{3,2,1,0:T(8,128)(2,1)} %get-tuple-element.12), channel_id=1, source_target_pairs={{0,8},{8,16},{16,24},{24,32},{32,40},{40,48},{48,56},{56,64},{64,7... | collective-permute-start | bytes 786440 | tf_op jit(solution)/shard_map/ppermute | solution.py:27
  201.4 9.4 %collective-permute-start.14 = (f32[128]{0:T(128)S(1)}, f32[128]{0:T(128)S(1)}, u32[]{:S(2)}, u32[]{:S(2)}) collective-permute-start(f32[128]{0:T(128)S(1)} %collective-permute-done.13), channel_id=1, source_target_pairs={{1,0},{2,1},{3,2},{4,3},{5,4},{6,5},{7,6},{0,7},{9,8},{10,9},{11,1... | collective-permute-start | bytes 1544 | tf_op jit(solution)/shard_map/ppermute | solution.py:125
  204.7 6.7 %collective-permute-start.11 = (f32[128]{0:T(128)S(1)}, f32[128]{0:T(128)S(1)}, u32[]{:S(2)}, u32[]{:S(2)}) collective-permute-start(f32[128]{0:T(128)S(1)} %collective-permute-done.10), channel_id=1, source_target_pairs={{0,1},{1,2},{2,3},{3,4},{4,5},{5,6},{6,7},{7,0},{8,9},{9,10},{10,1... | collective-permute-start | bytes 1544 | tf_op jit(solution)/shard_map/ppermute | solution.py:123
  208.6 3.4 copy-start
  213.5 199.1 %reduce-scatter.4.cloned.1.call-start = ((), (), s32[]{:S(2)}) async-start(), calls=%async_computation.3 | async-start | bytes 1064960
Sparse Core Ops, SparseCore 0:
  46.6 66.4 all-gather.4
  213.6 45.7 all-gather.2
  263.9 148.5 reduce-scatter.3
